TPU v7x, 128 devices: a whole 4x4x4 slice. The times are simulated.
128 devices in a mesh: mode: 8 (over x, core), member: 16 (over z, y).
Axes of the slice: x: 4, y: 4, z: 4, core: 2. Of those that a mesh axis runs over, the one named last changes fastest.
Arguments:
- ground_accel: bfloat16 [4, 639], replicated, may hold values from -6 to 6
- modal_kernel: bfloat16 [4096, 512], P(('mode', 'member')), may hold values from -0.25 to 0.25
- mode_shapes: bfloat16 [98304, 4096], P('member', 'mode'), may hold values from -0.09375 to 0.09375
- member_owner: int32 [16384, 1], P('member'), may hold values from 0 to 127; in each aligned block of 128 rows (0 to 127, 128 to 255, ...) at most 2 rows name the same one
- member_group: int32 [16384, 1], P('member'), may hold values from 0 to 3
- record_table: int32 [512, 8], P(('mode', 'member')), may hold values from 0 to 3
- case_coef: float32 [8, 6], replicated, may hold values from -1.5 to 1.5
- gravity: float32 [512, 8], P(('mode', 'member')), may hold values from -10 to 10
Outputs:
- demand: float32 [512, 8], P(('mode', 'member'))
Inputs may be any that keep to these rules, and one draw needn't show every extreme that they name: `member_owner`: in each aligned block of 1024 / 8 members no owner is named more than 2 times, a bound that some block reaches.
All inputs are finite; a program needn't handle non-finite values.
Results may differ from a plain program's by a relative error of at most 0.0065.
Values may be sent and summed in bfloat16 or wider, within the bound.
No kernel may reach another device: no remote copies, remote signals or barrier semaphores. Data moves between devices by JAX's collectives and lax.ppermute only.
A program may use at most 64 MiB of HBM per device.

v0:
```python
import jax
import jax.numpy as jnp
from jax import lax
from jax.sharding import PartitionSpec as P


def lagged_table(ground_accel, tap_count):
    record_count, span_len = ground_accel.shape
    step_count = span_len - tap_count + 1
    offsets = tap_count - 1 + jnp.arange(step_count)[None, :] - jnp.arange(tap_count)[:, None]
    lag_table = ground_accel[:, offsets]
    return jnp.transpose(lag_table, (1, 0, 2)).reshape(tap_count, record_count * step_count)


def local(
    ground_accel,
    modal_kernel,
    mode_shapes,
    member_owner,
    member_group,
    record_table,
    case_coef,
    gravity,
):
    tap_count = modal_kernel.shape[1]
    record_count = ground_accel.shape[0]
    comp_count = case_coef.shape[1]
    group_count = gravity.shape[0]
    n_mode = lax.axis_size("mode")
    n_member = lax.axis_size("member")
    lagged = lagged_table(ground_accel, tap_count)
    local_resp = jnp.dot(modal_kernel, lagged, preferred_element_type=jnp.float32).astype(
        jnp.bfloat16
    )
    modal_resp = lax.all_gather(local_resp, "member", axis=0, tiled=True)
    own_rows = mode_shapes.shape[0] // n_mode
    forces = lax.psum_scatter(
        jnp.dot(mode_shapes, modal_resp, preferred_element_type=jnp.float32).astype(jnp.bfloat16),
        "mode",
        scatter_dimension=0,
        tiled=True,
    ).astype(jnp.float32)
    members_here = own_rows // comp_count
    owner_total = n_mode * n_member
    slot_depth = max(2, 2 * members_here // owner_total)
    packed = forces.reshape(members_here, comp_count * forces.shape[1])
    first_row = lax.axis_index("mode") * members_here
    owner_ids = lax.dynamic_slice_in_dim(member_owner[:, 0], first_row, members_here)
    group_ids = lax.dynamic_slice_in_dim(member_group[:, 0], first_row, members_here)
    position = jnp.arange(members_here)
    earlier = (owner_ids[:, None] == owner_ids[None, :]) & (position[None, :] < position[:, None])
    member_rank = jnp.sum(earlier.astype(jnp.int32), axis=1)
    slot_index = owner_ids * slot_depth + member_rank
    slot_total = owner_total * slot_depth
    placement = jnp.arange(slot_total)[:, None] == slot_index[None, :]
    outgoing = jnp.dot(placement.astype(jnp.float32), packed, precision=lax.Precision.HIGHEST)
    slot_labels = jnp.max(jnp.where(placement, group_ids[None, :], -1), axis=1)
    incoming, slot_tags = (
        lax.all_to_all(
            outgoing.reshape(owner_total, slot_depth, -1).astype(jnp.bfloat16),
            ("mode", "member"),
            split_axis=0,
            concat_axis=0,
            tiled=True,
        ).astype(jnp.float32),
        lax.all_to_all(
            slot_labels.reshape(owner_total, slot_depth),
            ("mode", "member"),
            split_axis=0,
            concat_axis=0,
            tiled=True,
        ),
    )
    selector = (jnp.arange(group_count)[:, None] == slot_tags.reshape(-1)[None, :]).astype(
        jnp.float32
    )
    group_sums = jnp.dot(
        selector, incoming.reshape(selector.shape[1], -1), precision=lax.Precision.HIGHEST
    )
    group_sums = group_sums.reshape(group_count, comp_count, record_count, -1)
    case_mix = jnp.einsum("sc,gcrt->gsrt", case_coef, group_sums, precision=lax.Precision.HIGHEST)
    record_pick = (record_table[:, :, None] == jnp.arange(record_count)[None, None, :]).astype(
        jnp.float32
    )
    selected = jnp.sum(record_pick[:, :, :, None] * case_mix, axis=2)
    combined = gravity[:, :, None] + selected
    return jnp.max(jnp.abs(combined), axis=2)


def solution(mesh):
    placed = (
        P(),
        P(("mode", "member"), None),
        P("member", "mode"),
        P("member", None),
        P("member", None),
        P(("mode", "member"), None),
        P(),
        P(("mode", "member"), None),
    )
    return jax.shard_map(
        local, mesh=mesh, in_specs=placed, out_specs=P(("mode", "member"), None), check_vma=False
    )
```

profile of v0, /device:TPU:1, one launch (start us, length us, event | category | flops | bytes accessed | tf_op | source)
XLA Modules:
  0.0 376.7 jit_solution(7160551659993161368)
XLA Ops:
  6.5 0.9 copy.22
  7.5 227.3 %gather_fusion = bf16[65536,4]{1,0:T(8,128)(2,1)} fusion(bf16[4,639]{0,1:T(8,128)(2,1)S(1)} %copy.22, s32[65536]{0:T(1024)S(1)} %fusion.5), kind=kCustom, calls=%fused_computation | custom fusion | bytes 1310720 | tf_op jit(solution)/shard_map/gather | solution.py:11
  234.8 17.2 %copy.23 = bf16[512,128,4]{0,1,2:T(8,128)(2,1)S(1)} copy(bf16[512,128,4]{2,1,0:T(8,128)(2,1)} %bitcast.43) | data formatting | bytes 1048576 | tf_op jit(solution)/shard_map/gather | solution.py:11
  252.1 0.2 fusion.3
  252.3 21.2 %all_gather.3 = bf16[512,512]{1,0:T(8,128)(2,1)S(1)} all-gather(bf16[32,512]{1,0:T(8,128)(2,1)S(1)} %fusion.3), channel_id=1, replica_groups=mesh['mode'=8,'member'=16] {'member'}, dimensions={0}, use_global_device_ids=true | all-gather | bytes 557056 | tf_op jit(solution)/shard_map/all_gather | solution.py:35
  273.5 8.3 %fusion = bf16[6144,512]{0,1:T(8,128)(2,1)} fusion(bf16[512,512]{1,0:T(8,128)(2,1)S(1)} %all_gather.3, bf16[6144,512]{1,0:T(8,128)(2,1)} %param.10), kind=kOutput, calls=%fused_computation.2 | convolution fusion | flops 3224371200 | bytes 13107200 | tf_op jit(solution)/shard_map/dot_general | solution.py:38
  281.8 0.7 dynamic-slice_bitcast_fusion.1
  282.5 0.7 dynamic-slice_bitcast_fusion
  283.3 0.7 multiply_add_fusion.1
  284.1 0.8 all_to_all.9
  284.8 12.8 %all-to-all-start = ((s32[128,1,2]{2,1,0:T(1,128)}), s32[128,1,2]{2,1,0:T(1,128)S(1)}, u32[]{:S(2)}, u32[]{:S(2)}) async-start(s32[128,1,2]{2,1,0:T(1,128)} %bitcast.2), calls=%async_computation | async-start | bytes 131072 | tf_op jit(solution)/shard_map/all_to_all | solution.py:66
  297.6 31.4 %reduce-scatter.2.cloned.1.call-done = bf16[768,512]{0,1:T(8,128)(2,1)} async-done(((bf16[6144,512]{0,1:T(8,128)(2,1)}), bf16[768,512]{0,1:T(8,128)(2,1)}) %reduce-scatter.2.cloned.1.call-update) | async-done | bytes 786448 | tf_op jit(solution)/shard_map/reduce_scatter | solution.py:37
  329.0 1.4 copy.24
  330.4 0.7 reshape.112
  331.1 0.6 convolution_convert_fusion.1
  331.7 2.8 copy.25
  334.5 8.5 %all-to-all-start.1 = ((bf16[128,2,3072]{2,1,0:T(2,128)(2,1)}), bf16[128,2,3072]{2,1,0:T(2,128)(2,1)S(1)}, u32[]{:S(2)}, u32[]{:S(2)}) async-start(bf16[128,2,3072]{2,1,0:T(2,128)(2,1)} %copy.25), calls=%async_computation.2 | async-start | bytes 3145728 | tf_op jit(solution)/shard_map/all_to_all | solution.py:59
  343.0 0.5 broadcast.73
  343.5 0.8 reduce.3
  344.5 22.6 %all-to-all-done.1 = bf16[128,2,3072]{2,1,0:T(2,128)(2,1)S(1)} async-done(((bf16[128,2,3072]{2,1,0:T(2,128)(2,1)}), bf16[128,2,3072]{2,1,0:T(2,128)(2,1)S(1)}, u32[]{:S(2)}, u32[]{:S(2)}) %all-to-all-start.1) | async-done | bytes 1572896 | tf_op jit(solution)/shard_map/all_to_all | solution.py:59
  367.1 0.6 reshape.102
  367.7 0.7 copy.26
  368.4 0.5 fusion.14
  369.2 0.7 abs_reduce_fusion
  (19 shorter events, 0.8 us)
Async XLA Ops:
  6.5 245.6 %copy-start = (bf16[32,512]{1,0:T(8,128)(2,1)S(1)}, bf16[32,512]{1,0:T(8,128)(2,1)}, u32[]{:S(2)}) copy-start(bf16[32,512]{1,0:T(8,128)(2,1)} %param.9) | copy-start | bytes 98308
  6.5 322.5 %reduce-scatter.2.cloned.1.call-start = ((), (), s32[]{:S(2)}) async-start(), calls=%async_computation.3 | async-start | bytes 7077888 | tf_op jit(solution)/shard_map/reduce_scatter | solution.py:37
  281.8 61.2 %copy-start.1 = (s32[4,8]{1,0:T(4,128)S(1)}, s32[4,8]{1,0:T(4,128)}, u32[]{:S(2)}) copy-start(s32[4,8]{1,0:T(4,128)} %param.13) | copy-start | bytes 388
  284.8 49.6 %all-to-all-start = ((s32[128,1,2]{2,1,0:T(1,128)}), s32[128,1,2]{2,1,0:T(1,128)S(1)}, u32[]{:S(2)}, u32[]{:S(2)}) async-start(s32[128,1,2]{2,1,0:T(1,128)} %bitcast.2), calls=%async_computation | async-start | bytes 131072 | tf_op jit(solution)/shard_map/all_to_all | solution.py:66
  334.5 34.5 %copy-start.3 = (f32[8,6]{1,0:T(8,128)S(1)}, f32[8,6]{1,0:T(8,128)}, u32[]{:S(2)}) copy-start(f32[8,6]{1,0:T(8,128)} %param.14) | copy-start | bytes 580
  334.5 34.7 %copy-start.2 = (f32[4,8]{1,0:T(4,128)S(1)}, f32[4,8]{1,0:T(4,128)}, u32[]{:S(2)}) copy-start(f32[4,8]{1,0:T(4,128)} %param.15) | copy-start | bytes 388
  334.5 32.6 %all-to-all-start.1 = ((bf16[128,2,3072]{2,1,0:T(2,128)(2,1)}), bf16[128,2,3072]{2,1,0:T(2,128)(2,1)S(1)}, u32[]{:S(2)}, u32[]{:S(2)}) async-start(bf16[128,2,3072]{2,1,0:T(2,128)(2,1)} %copy.25), calls=%async_computation.2 | async-start | bytes 3145728 | tf_op jit(solution)/shard_map/all_to_all | solution.py:59
Sparse Core Ops, SparseCore 0:
  281.9 47.0 reduce-scatter.1
where the time goes:
time: 377 us
  local copies, waits for them, and re-layouts  254 us (67%)
  waiting for transfers between devices  54 us (14%)
  starting transfers between devices  21.3 us (6%)
  blocking collectives  21.2 us (6%)
  between operations  13.5 us (4%)
  matrix products  9.81 us (3%)
    gather x2, local copies, waits for them, and re-layouts, lagged_table(): lag_table = ground_accel[:, offsets]  245 us
    reduce_scatter x1, waiting for transfers between devices, local(): lax.psum_scatter(jnp.dot(mode_shapes, modal_resp, preferred_element_type=...  31.4 us
    all_to_all x1, waiting for transfers between devices, local(): lax.all_to_all(outgoing.reshape(owner_total, slot_depth, -1).astype(jnp.b...  22.6 us
    all_gather x1, blocking collectives, local(): modal_resp = lax.all_gather(local_resp, 'member', axis=0, tiled=True)  21.2 us
    all_to_all x1, starting transfers between devices, local(): lax.all_to_all(slot_labels.reshape(owner_total, slot_depth), ('mode', 'me...  12.8 us
    all_to_all x1, starting transfers between devices, local(): lax.all_to_all(outgoing.reshape(owner_total, slot_depth, -1).astype(jnp.b...  8.53 us
    dot_general x1, matrix products, local(): jnp.dot(mode_shapes, modal_resp, preferred_element_type=jnp.float32)  8.25 us
  transfers between devices with their start and end apart: 3, of which 2 were waited for; matrix products, arithmetic and copies ran while one was open for 2% of the time, Pallas kernels for 0%

commit v1 on v0

--- a/solution.py
+++ b/solution.py
@@ -2,6 +2,14 @@
 import jax.numpy as jnp
 from jax import lax
 from jax.sharding import PartitionSpec as P
+
+
+def gather_from_all(array, axis, dim):
+    devices = lax.axis_size(axis)
+    repeats = [devices if d == dim else 1 for d in range(array.ndim)]
+    return lax.all_to_all(
+        jnp.tile(array, repeats), axis, split_axis=dim, concat_axis=dim, tiled=True
+    )
 
 
 def lagged_table(ground_accel, tap_count):
@@ -32,7 +40,7 @@
     local_resp = jnp.dot(modal_kernel, lagged, preferred_element_type=jnp.float32).astype(
         jnp.bfloat16
     )
-    modal_resp = lax.all_gather(local_resp, "member", axis=0, tiled=True)
+    modal_resp = gather_from_all(local_resp, "member", 0)
     own_rows = mode_shapes.shape[0] // n_mode
     forces = lax.psum_scatter(
         jnp.dot(mode_shapes, modal_resp, preferred_element_type=jnp.float32).astype(jnp.bfloat16),

time: 377 us -> 370 us (0.981)
  starting transfers between devices: 21.3 us -> 15.6 us
    all_gather x1 -> x0, blocking collectives: 21.2 us -> none  [local(): modal_resp = lax.all_gather(local_resp, 'member', axis=0, tiled=True)]
    all_to_all x0 -> x1, blocking collectives: none -> 18.9 us  [gather_from_all(): lax.all_to_all(jnp.tile(array, repeats), axis, split_axis=dim, concat_axi...]
    all_to_all x1, starting transfers between devices: 12.8 us -> 7.07 us  [local(): lax.all_to_all(slot_labels.reshape(owner_total, slot_depth), ('mode', 'me...]
where the time goes in v1:
time: 370 us; the launch traced here: 369 us
  local copies, waits for them, and re-layouts  254 us (69%)
  waiting for transfers between devices  54 us (15%)
  blocking collectives  18.9 us (5%)
  starting transfers between devices  15.6 us (4%)
  between operations  13.5 us (4%)
  matrix products  9.81 us (3%)
    gather x2, local copies, waits for them, and re-layouts, lagged_table(): lag_table = ground_accel[:, offsets]  245 us
    reduce_scatter x1, waiting for transfers between devices, local(): lax.psum_scatter(jnp.dot(mode_shapes, modal_resp, preferred_element_type=...  31.4 us
    all_to_all x1, waiting for transfers between devices, local(): lax.all_to_all(outgoing.reshape(owner_total, slot_depth, -1).astype(jnp.b...  22.6 us
    all_to_all x1, blocking collectives, gather_from_all(): lax.all_to_all(jnp.tile(array, repeats), axis, split_axis=dim, concat_axi...  18.9 us
    all_to_all x1, starting transfers between devices, local(): lax.all_to_all(outgoing.reshape(owner_total, slot_depth, -1).astype(jnp.b...  8.5 us
    dot_general x1, matrix products, local(): jnp.dot(mode_shapes, modal_resp, preferred_element_type=jnp.float32)  8.24 us
  transfers between devices with their start and end apart: 3, of which 2 were waited for; matrix products, arithmetic and copies ran while one was open for 2% of the time, Pallas kernels for 0%

profile of v1, /device:TPU:1, one launch (start us, length us, event | category | flops | bytes accessed | tf_op | source)
XLA Modules:
  0.0 368.8 jit_solution(18380344585858045743)
XLA Ops:
  6.5 0.9 copy.22
  7.5 227.3 %gather_fusion = bf16[65536,4]{1,0:T(8,128)(2,1)} fusion(bf16[4,639]{0,1:T(8,128)(2,1)S(1)} %copy.22, s32[65536]{0:T(1024)S(1)} %fusion.5), kind=kCustom, calls=%fused_computation | custom fusion | bytes 1310720 | tf_op jit(solution)/shard_map/gather | solution.py:19
  234.8 17.2 %copy.23 = bf16[512,128,4]{0,1,2:T(8,128)(2,1)S(1)} copy(bf16[512,128,4]{2,1,0:T(8,128)(2,1)} %bitcast.44) | data formatting | bytes 1048576 | tf_op jit(solution)/shard_map/gather | solution.py:19
  252.1 0.2 fusion.3
  252.4 18.9 %all_to_all.23 = bf16[16,32,512]{2,1,0:T(8,128)(2,1)S(1)} all-to-all(bf16[16,32,512]{2,1,0:T(8,128)(2,1)S(1)} %tile.2), channel_id=1, replica_groups=mesh['mode'=8,'member'=16] {'member'}, dimensions={0} | all-to-all | bytes 1048576 | tf_op jit(solution)/shard_map/all_to_all | solution.py:10
  271.3 8.2 %fusion = bf16[6144,512]{0,1:T(8,128)(2,1)} fusion(bf16[512,512]{1,0:T(8,128)(2,1)S(1)} %bitcast.48, bf16[6144,512]{1,0:T(8,128)(2,1)} %param.10), kind=kOutput, calls=%fused_computation.2 | convolution fusion | flops 3224371200 | bytes 13107200 | tf_op jit(solution)/shard_map/dot_general | solution.py:46
  279.6 0.7 dynamic-slice_bitcast_fusion.1
  280.3 0.7 dynamic-slice_bitcast_fusion
  281.1 0.7 multiply_add_fusion.1
  281.9 0.8 all_to_all.15
  282.6 7.1 %all-to-all-start = ((s32[128,1,2]{2,1,0:T(1,128)}), s32[128,1,2]{2,1,0:T(1,128)S(1)}, u32[]{:S(2)}, u32[]{:S(2)}) async-start(s32[128,1,2]{2,1,0:T(1,128)} %bitcast.2), calls=%async_computation | async-start | bytes 131072 | tf_op jit(solution)/shard_map/all_to_all | solution.py:74
  289.7 31.4 %reduce-scatter.2.cloned.1.call-done = bf16[768,512]{0,1:T(8,128)(2,1)} async-done(((bf16[6144,512]{0,1:T(8,128)(2,1)}), bf16[768,512]{0,1:T(8,128)(2,1)}) %reduce-scatter.2.cloned.1.call-update) | async-done | bytes 786448 | tf_op jit(solution)/shard_map/reduce_scatter | solution.py:45
  321.1 1.4 copy.24
  322.5 0.7 reshape.119
  323.2 0.6 convolution_convert_fusion.1
  323.8 2.8 copy.25
  326.6 8.5 %all-to-all-start.2 = ((bf16[128,2,3072]{2,1,0:T(2,128)(2,1)}), bf16[128,2,3072]{2,1,0:T(2,128)(2,1)S(1)}, u32[]{:S(2)}, u32[]{:S(2)}) async-start(bf16[128,2,3072]{2,1,0:T(2,128)(2,1)} %copy.25), calls=%async_computation.3 | async-start | bytes 3145728 | tf_op jit(solution)/shard_map/all_to_all | solution.py:67
  335.1 0.5 broadcast.76
  335.7 0.8 reduce.3
  336.6 22.6 %all-to-all-done.2 = bf16[128,2,3072]{2,1,0:T(2,128)(2,1)S(1)} async-done(((bf16[128,2,3072]{2,1,0:T(2,128)(2,1)}), bf16[128,2,3072]{2,1,0:T(2,128)(2,1)S(1)}, u32[]{:S(2)}, u32[]{:S(2)}) %all-to-all-start.2) | async-done | bytes 1572896 | tf_op jit(solution)/shard_map/all_to_all | solution.py:67
  359.2 0.6 reshape.109
  359.8 0.7 copy.26
  360.5 0.5 fusion.14
  361.3 0.7 abs_reduce_fusion
  (20 shorter events, 0.8 us)
Async XLA Ops:
  6.5 245.6 %copy-start = (bf16[32,512]{1,0:T(8,128)(2,1)S(1)}, bf16[32,512]{1,0:T(8,128)(2,1)}, u32[]{:S(2)}) copy-start(bf16[32,512]{1,0:T(8,128)(2,1)} %param.9) | copy-start | bytes 98308
  6.5 314.6 %reduce-scatter.2.cloned.1.call-start = ((), (), s32[]{:S(2)}) async-start(), calls=%async_computation.4 | async-start | bytes 7077888 | tf_op jit(solution)/shard_map/reduce_scatter | solution.py:45
  279.6 55.5 %copy-start.1 = (s32[4,8]{1,0:T(4,128)S(1)}, s32[4,8]{1,0:T(4,128)}, u32[]{:S(2)}) copy-start(s32[4,8]{1,0:T(4,128)} %param.13) | copy-start | bytes 388
  282.6 44.0 %all-to-all-start = ((s32[128,1,2]{2,1,0:T(1,128)}), s32[128,1,2]{2,1,0:T(1,128)S(1)}, u32[]{:S(2)}, u32[]{:S(2)}) async-start(s32[128,1,2]{2,1,0:T(1,128)} %bitcast.2), calls=%async_computation | async-start | bytes 131072 | tf_op jit(solution)/shard_map/all_to_all | solution.py:74
  326.6 34.4 %copy-start.3 = (f32[8,6]{1,0:T(8,128)S(1)}, f32[8,6]{1,0:T(8,128)}, u32[]{:S(2)}) copy-start(f32[8,6]{1,0:T(8,128)} %param.14) | copy-start | bytes 580
  326.6 34.7 %copy-start.2 = (f32[4,8]{1,0:T(4,128)S(1)}, f32[4,8]{1,0:T(4,128)}, u32[]{:S(2)}) copy-start(f32[4,8]{1,0:T(4,128)} %param.15) | copy-start | bytes 388
  326.6 32.6 %all-to-all-start.2 = ((bf16[128,2,3072]{2,1,0:T(2,128)(2,1)}), bf16[128,2,3072]{2,1,0:T(2,128)(2,1)S(1)}, u32[]{:S(2)}, u32[]{:S(2)}) async-start(bf16[128,2,3072]{2,1,0:T(2,128)(2,1)} %copy.25), calls=%async_computation.3 | async-start | bytes 3145728 | tf_op jit(solution)/shard_map/all_to_all | solution.py:67
Sparse Core Ops, SparseCore 0:
  279.7 41.3 reduce-scatter.1
